TPU v7x, 512 devices: a whole 4x4x16 slice. The times are simulated.
512 devices in a mesh: seq: 128 (over y, z, core), head: 4 (over x).
Axes of the slice: x: 4, y: 4, z: 16, core: 2. Of those that a mesh axis runs over, the one named last changes fastest.
Arguments:
- tokens: bfloat16 [64, 4, 1024], P('head'), may hold values from -6 to 6
- cache_keys: bfloat16 [64, 4096, 512], P(None, 'seq', 'head'), may hold values from -70 to 70
- cache_values: bfloat16 [64, 4096, 512], P(None, 'seq', 'head'), may hold values from -6 to 6
- held_states: bfloat16 [64, 512, 1024], P(None, 'seq'), may hold values from -6 to 6
- recompute_pos: int32 [64, 512], P(None, 'seq'), may hold values from 0 to 4095, as said below
- cache_len: int32 [64], replicated, may hold values from 1 to 4096
- new_prompt: int32 [64], replicated, may hold values 0 or 1
- w_qkv: bfloat16 [3, 1024, 512], P(None, None, 'head'), may hold values from -0.1875 to 0.1875
- qkv_bias: float32 [3, 512], P(None, 'head'), may hold values from -3 to 3
- w_out: bfloat16 [512, 1024], P('head'), may hold values from -1.5 to 1.5
- out_bias: float32 [1024], replicated, may hold values from -3 to 3
- attn_gain: float32 [1024], replicated, may hold values from 0.1 to 1.9
- attn_shift: float32 [1024], replicated, may hold values from -3 to 3
- w_up: bfloat16 [1024, 2048], P(None, 'head'), may hold values from -0.1875 to 0.1875
- up_bias: float32 [2048], P('head'), may hold values from -3 to 3
- w_down: bfloat16 [2048, 1024], P('head'), may hold values from -0.125 to 0.125
- down_bias: float32 [1024], replicated, may hold values from -3 to 3
- ffn_gain: float32 [1024], replicated, may hold values from 0.1 to 1.9
- ffn_shift: float32 [1024], replicated, may hold values from -3 to 3
Outputs:
- layer_out: bfloat16 [64, 4, 1024], P('head')
Inputs may be any that keep to these rules, and one draw needn't show every extreme that they name: `recompute_pos`: columns s * 4 to (s + 1) * 4 - 1 of a row hold distinct positions from s * 32 to (s + 1) * 32 - 1.
All inputs are finite; a program needn't handle non-finite values.
Results may differ from a plain program's by a relative error of at most 0.011.
Values may be sent and summed in bfloat16 or wider, within the bound.
No kernel may reach another device: no remote copies, remote signals or barrier semaphores. Data moves between devices by JAX's collectives and lax.ppermute only.
A program may use at most 192 MiB of HBM per device.

v0:
```python
import jax
import jax.numpy as jnp
from jax import lax
from jax.sharding import PartitionSpec as P

HDIM = 64
NEG = -1e30
EPS = 1e-05


def layer_norm(values, norm_gain, norm_bias):
    center = jnp.mean(values, axis=-1, keepdims=True)
    spread = values - center
    second = jnp.mean(spread * spread, axis=-1, keepdims=True)
    return spread * lax.rsqrt(second + EPS) * norm_gain + norm_bias


def merge_pair(first_part, second_part):
    first_max, first_sum, first_out = first_part
    second_max, second_sum, second_out = second_part
    joint_max = jnp.maximum(first_max, second_max)
    first_scale = jnp.exp(first_max - joint_max)
    second_scale = jnp.exp(second_max - joint_max)
    return (
        joint_max,
        first_sum * first_scale + second_sum * second_scale,
        first_out * first_scale[..., None] + second_out * second_scale[..., None],
    )


def partial_attention(queries, keys_here, values_here, visible):
    scores = jnp.einsum(
        "rthe,rphe->rthp", queries, keys_here, preferred_element_type=jnp.float32
    ) * HDIM ** (-0.5)
    highest = jnp.max(jnp.where(visible, scores, NEG), axis=-1)
    weights = jnp.exp(jnp.where(visible, scores - highest[..., None], NEG)).astype(jnp.bfloat16)
    totals = jnp.sum(weights.astype(jnp.float32), axis=-1)
    blended = jnp.einsum(
        "rthp,rphe->rthe", weights, values_here, preferred_element_type=jnp.float32
    )
    return (highest, totals, blended)


def seq_merge(block_max, block_sum, block_out):
    n_seq = lax.axis_size("seq")
    head_shape = block_out.shape
    lanes = head_shape[-2] * head_shape[-1]
    rows = block_out.size // lanes
    stat_rows = block_max.size // lanes
    out2 = block_out.reshape(rows, lanes)
    top = block_max.reshape(stat_rows, lanes)
    total = block_sum.reshape(stat_rows, lanes)
    width = head_shape[-1]
    step = 1
    while step < n_seq:
        pairs = [(i, i ^ step) for i in range(n_seq)]
        packed = jnp.concatenate([out2, top, total], axis=0)
        other = lax.ppermute(packed, "seq", pairs)
        o_out = other[:rows]
        o_top = other[rows : rows + stat_rows]
        o_total = other[rows + stat_rows :]
        joint = jnp.maximum(top, o_top)
        mine = jnp.exp(top - joint)
        theirs = jnp.exp(o_top - joint)
        total = total * mine + o_total * theirs
        mine_rows = jnp.repeat(mine.reshape(rows, lanes // width), width, axis=1)
        theirs_rows = jnp.repeat(theirs.reshape(rows, lanes // width), width, axis=1)
        out2 = out2 * mine_rows + o_out * theirs_rows
        top = joint
        step *= 2
    return (top.reshape(block_max.shape), total.reshape(block_sum.shape), out2.reshape(head_shape))


def on_device(
    tokens,
    cache_keys,
    cache_values,
    held_states,
    recompute_pos,
    cache_len,
    new_prompt,
    w_qkv,
    qkv_bias,
    w_out,
    out_bias,
    attn_gain,
    attn_shift,
    w_up,
    up_bias,
    w_down,
    down_bias,
    ffn_gain,
    ffn_shift,
):
    local_width = w_qkv.shape[2]
    local_heads = local_width // HDIM
    requests = cache_keys.shape[0]
    block_len = cache_keys.shape[1]
    own_rows = tokens.shape[0]
    steps_count = tokens.shape[1]
    block_rows = lax.all_gather(tokens, "head", axis=0, tiled=True)
    triple = (
        jnp.einsum("rtd,kdc->rtkc", block_rows, w_qkv, preferred_element_type=jnp.float32)
        + qkv_bias
    )
    triple = triple.astype(jnp.bfloat16).reshape(
        block_rows.shape[0], block_rows.shape[1], 3 * local_width
    )
    gathered = jnp.concatenate([triple, block_rows], axis=2)
    head_shape = (requests, steps_count, local_heads, HDIM)
    queries = gathered[:, :, :local_width].reshape(head_shape)
    new_keys = gathered[:, :, local_width : 2 * local_width].reshape(head_shape)
    new_values = gathered[:, :, 2 * local_width : 3 * local_width].reshape(head_shape)
    fresh_keys = (
        jnp.einsum("rjd,dc->rjc", held_states, w_qkv[1], preferred_element_type=jnp.float32)
        + qkv_bias[1]
    ).astype(jnp.bfloat16)
    offset_pos = lax.axis_index("seq") * block_len
    positions = jnp.arange(block_len, dtype=jnp.int32)
    matches = (recompute_pos - offset_pos)[:, :, None] == positions[None, None, :]
    placed = jnp.einsum(
        "rjp,rjc->rpc", matches.astype(jnp.bfloat16), fresh_keys, preferred_element_type=jnp.float32
    ).astype(jnp.bfloat16)
    replaced = jnp.any(matches, axis=1)
    keys_here = jnp.where(replaced[:, :, None], placed, cache_keys).reshape(
        requests, block_len, local_heads, HDIM
    )
    values_here = cache_values.reshape(requests, block_len, local_heads, HDIM)
    visible = ((offset_pos + positions)[None, :] < cache_len[:, None]) & (new_prompt[:, None] == 0)
    block_max, block_sum, block_out = partial_attention(
        queries, keys_here, values_here, visible[:, None, None, :]
    )
    cache_max, cache_sum, cache_out = seq_merge(block_max, block_sum, block_out)
    order_t = jnp.arange(steps_count, dtype=jnp.int32)
    causal = (order_t[:, None] >= order_t[None, :])[None, :, None, :]
    new_max, new_sum, new_out = partial_attention(queries, new_keys, new_values, causal)
    joint_max, joint_sum, joint_out = merge_pair(
        (cache_max, cache_sum, cache_out), (new_max, new_sum, new_out)
    )
    attended = (
        (joint_out / joint_sum[..., None])
        .astype(jnp.bfloat16)
        .reshape(requests, steps_count, local_width)
    )
    head_terms = jnp.einsum("rtc,cd->rtd", attended, w_out, preferred_element_type=jnp.float32)
    summed = lax.psum(head_terms, "head")
    inputs_all = gathered[:, :, 3 * local_width :]
    normed_all = layer_norm(
        inputs_all.astype(jnp.float32) + summed + out_bias, attn_gain, attn_shift
    ).astype(jnp.bfloat16)
    hidden_all = jax.nn.gelu(
        jnp.einsum("rtd,df->rtf", normed_all, w_up, preferred_element_type=jnp.float32) + up_bias,
        approximate=False,
    ).astype(jnp.bfloat16)
    normed = lax.dynamic_slice_in_dim(normed_all, lax.axis_index("head") * own_rows, own_rows, 0)
    reduced = lax.psum_scatter(
        jnp.einsum("rtf,fd->rtd", hidden_all, w_down, preferred_element_type=jnp.float32),
        "head",
        scatter_dimension=0,
        tiled=True,
    )
    return layer_norm(normed.astype(jnp.float32) + reduced + down_bias, ffn_gain, ffn_shift).astype(
        jnp.bfloat16
    )


def solution(mesh):
    placed = (
        P("head", None, None),
        P(None, "seq", "head"),
        P(None, "seq", "head"),
        P(None, "seq", None),
        P(None, "seq"),
        P(),
        P(),
        P(None, None, "head"),
        P(None, "head"),
        P("head", None),
        P(),
        P(),
        P(),
        P(None, "head"),
        P("head"),
        P("head", None),
        P(),
        P(),
        P(),
    )
    return jax.shard_map(
        on_device, mesh=mesh, in_specs=placed, out_specs=P("head", None, None), check_vma=False
    )
```

profile of v0, /device:TPU:8, one launch (start us, length us, event | category | flops | bytes accessed | tf_op | source)
XLA Modules:
  0.0 232.6 jit_solution(7463980318247415298)
XLA Ops:
  9.0 1.0 copy.122
  10.0 13.1 %all_gather.3 = bf16[64,4,1024]{2,0,1:T(8,128)(2,1)S(1)} all-gather(bf16[16,4,1024]{2,0,1:T(8,128)(2,1)S(1)} %copy.122), channel_id=1, replica_groups=mesh['seq'=128,'head'=4] {'head'}, dimensions={0}, use_global_device_ids=true | all-gather | bytes 655360 | tf_op jit(solution)/shard_map/all_gather | solution.py:101
  27.7 1.7 select_reduce_fusion
  32.4 1.9 collective-permute-start
  34.3 1.3 collective-permute-done
  36.4 3.8 %collective-permute-start.1 = (f32[264,128]{1,0:T(8,128)S(1)}, f32[264,128]{1,0:T(8,128)S(1)}, u32[]{:S(2)}, u32[]{:S(2)}) collective-permute-start(f32[264,128]{1,0:T(8,128)S(1)} %pad_maximum_fusion.1), channel_id=1, source_target_pairs={{0,8},{4,12},{8,0},{12,4},{16,24},{20,28},{24,16},{28,20},{32,40},... | collective-permute-start | bytes 405512 | tf_op jit(solution)/shard_map/ppermute | solution.py:58
  40.3 3.9 %collective-permute-done.1 = f32[264,128]{1,0:T(8,128)S(1)} collective-permute-done((f32[264,128]{1,0:T(8,128)S(1)}, f32[264,128]{1,0:T(8,128)S(1)}, u32[]{:S(2)}, u32[]{:S(2)}) %collective-permute-start.1) | collective-permute-done | bytes 135200 | tf_op jit(solution)/shard_map/ppermute | solution.py:58
  44.9 5.2 %collective-permute-start.2 = (f32[264,128]{1,0:T(8,128)S(1)}, f32[264,128]{1,0:T(8,128)S(1)}, u32[]{:S(2)}, u32[]{:S(2)}) collective-permute-start(f32[264,128]{1,0:T(8,128)S(1)} %pad_maximum_fusion.2), channel_id=1, source_target_pairs={{0,16},{4,20},{8,24},{12,28},{16,0},{20,4},{24,8},{28,12},{32,48},... | collective-permute-start | bytes 405512 | tf_op jit(solution)/shard_map/ppermute | solution.py:58
  50.1 6.1 %collective-permute-done.2 = f32[264,128]{1,0:T(8,128)S(1)} collective-permute-done((f32[264,128]{1,0:T(8,128)S(1)}, f32[264,128]{1,0:T(8,128)S(1)}, u32[]{:S(2)}, u32[]{:S(2)}) %collective-permute-start.2) | collective-permute-done | bytes 135200 | tf_op jit(solution)/shard_map/ppermute | solution.py:58
  57.0 9.1 %collective-permute-start.3 = (f32[264,128]{1,0:T(8,128)S(1)}, f32[264,128]{1,0:T(8,128)S(1)}, u32[]{:S(2)}, u32[]{:S(2)}) collective-permute-start(f32[264,128]{1,0:T(8,128)S(1)} %pad_maximum_fusion.3), channel_id=1, source_target_pairs={{0,32},{4,36},{8,40},{12,44},{16,48},{20,52},{24,56},{28,60},{32,0... | collective-permute-start | bytes 405512 | tf_op jit(solution)/shard_map/ppermute | solution.py:58
  66.2 10.2 %collective-permute-done.3 = f32[264,128]{1,0:T(8,128)S(1)} collective-permute-done((f32[264,128]{1,0:T(8,128)S(1)}, f32[264,128]{1,0:T(8,128)S(1)}, u32[]{:S(2)}, u32[]{:S(2)}) %collective-permute-start.3) | collective-permute-done | bytes 135200 | tf_op jit(solution)/shard_map/ppermute | solution.py:58
  77.1 13.6 %collective-permute-start.4 = (f32[264,128]{1,0:T(8,128)S(1)}, f32[264,128]{1,0:T(8,128)S(1)}, u32[]{:S(2)}, u32[]{:S(2)}) collective-permute-start(f32[264,128]{1,0:T(8,128)S(1)} %pad_maximum_fusion.4), channel_id=1, source_target_pairs={{0,64},{4,68},{8,72},{12,76},{16,80},{20,84},{24,88},{28,92},{32,9... | collective-permute-start | bytes 405512 | tf_op jit(solution)/shard_map/ppermute | solution.py:58
  91.0 12.1 %collective-permute-done.4 = f32[264,128]{1,0:T(8,128)S(1)} collective-permute-done((f32[264,128]{1,0:T(8,128)S(1)}, f32[264,128]{1,0:T(8,128)S(1)}, u32[]{:S(2)}, u32[]{:S(2)}) %collective-permute-start.4) | collective-permute-done | bytes 135200 | tf_op jit(solution)/shard_map/ppermute | solution.py:58
  103.9 3.5 %collective-permute-start.5 = (f32[264,128]{1,0:T(8,128)S(1)}, f32[264,128]{1,0:T(8,128)S(1)}, u32[]{:S(2)}, u32[]{:S(2)}) collective-permute-start(f32[264,128]{1,0:T(8,128)S(1)} %pad_maximum_fusion.5), channel_id=1, source_target_pairs={{0,128},{4,132},{8,136},{12,140},{16,144},{20,148},{24,152},{28,15... | collective-permute-start | bytes 405512 | tf_op jit(solution)/shard_map/ppermute | solution.py:58
  107.8 3.3 %collective-permute-done.5 = f32[264,128]{1,0:T(8,128)S(1)} collective-permute-done((f32[264,128]{1,0:T(8,128)S(1)}, f32[264,128]{1,0:T(8,128)S(1)}, u32[]{:S(2)}, u32[]{:S(2)}) %collective-permute-start.5) | collective-permute-done | bytes 135200 | tf_op jit(solution)/shard_map/ppermute | solution.py:58
  111.9 3.9 %collective-permute-start.6 = (f32[264,128]{1,0:T(8,128)S(1)}, f32[264,128]{1,0:T(8,128)S(1)}, u32[]{:S(2)}, u32[]{:S(2)}) collective-permute-start(f32[264,128]{1,0:T(8,128)S(1)} %pad_maximum_fusion.6), channel_id=1, source_target_pairs={{0,256},{4,260},{8,264},{12,268},{16,272},{20,276},{24,280},{28,28... | collective-permute-start | bytes 405512 | tf_op jit(solution)/shard_map/ppermute | solution.py:58
  116.1 4.2 %collective-permute-done.6 = f32[264,128]{1,0:T(8,128)S(1)} collective-permute-done((f32[264,128]{1,0:T(8,128)S(1)}, f32[264,128]{1,0:T(8,128)S(1)}, u32[]{:S(2)}, u32[]{:S(2)}) %collective-permute-start.6) | collective-permute-done | bytes 135200 | tf_op jit(solution)/shard_map/ppermute | solution.py:58
  123.7 1.3 fusion.29
  125.3 58.1 %all-reduce.2.cloned.1.call-done = f32[64,4,1024]{2,0,1:T(8,128)} async-done(((f32[64,4,1024]{2,0,1:T(8,128)}), f32[64,4,1024]{2,0,1:T(8,128)}) %all-reduce.2.cloned.1.call-update) | async-done | bytes 1048592 | tf_op jit(solution)/shard_map/psum | solution.py:146
  183.4 1.5 fusion.26
  186.3 0.9 copy-done.16
  187.8 2.5 %fusion.9 = f32[64,4,1024]{2,0,1:T(8,128)} fusion(bf16[512,1024]{1,0:T(8,128)(2,1)S(1)} %copy-done, f32[64,4,512]{2,0,1:T(8,128)S(1)} %get-tuple-element.45, u8[64,512]{1,0:T(8,128)(4,1)S(1)} %get-tuple-element.6, u8[64,512]{1,0:T(8,128)(4,1)S(1)} %get-tuple-element.5), kind=kOutput, calls=%fused_computation.16 | convolution fusion | flops 277610496 | bytes 2686976 | tf_op jit(solution)/shard_map/rtf,fd->rtd/dot_general | solution.py:157
  190.3 32.6 %reduce-scatter.2.cloned.1.call-done = f32[16,4,1024]{2,0,1:T(8,128)} async-done(((f32[64,4,1024]{2,0,1:T(8,128)}), f32[16,4,1024]{2,0,1:T(8,128)}) %reduce-scatter.2.cloned.1.call-update) | async-done | bytes 262160 | tf_op jit(solution)/shard_map/reduce_scatter | solution.py:156
  222.9 1.1 fusion.82
  (173 shorter events, 22.4 us)
Async XLA Ops:
  6.5 181.2 %copy-start = (bf16[512,1024]{1,0:T(8,128)(2,1)S(1)}, bf16[512,1024]{1,0:T(8,128)(2,1)}, u32[]{:S(2)}) copy-start(bf16[512,1024]{1,0:T(8,128)(2,1)} %param.34) | copy-start | bytes 3145732
  6.5 16.6 %copy-start.3 = (bf16[3,1024,128]{2,1,0:T(8,128)(2,1)S(1)}, bf16[3,1024,128]{2,1,0:T(8,128)(2,1)}, u32[]{:S(2)}) copy-start(bf16[3,1024,128]{2,1,0:T(8,128)(2,1)} %param.26) | copy-start | bytes 2359300
  6.5 176.9 %all-reduce.2.cloned.1.call-start = ((), (), s32[]{:S(2)}) async-start(), calls=%async_computation.1 | async-start | bytes 2097152 | tf_op jit(solution)/shard_map/psum | solution.py:146
  9.9 13.2 %copy-start.14 = (f32[3,128]{1,0:T(4,128)S(1)}, f32[3,128]{1,0:T(4,128)}, u32[]{:S(2)}) copy-start(f32[3,128]{1,0:T(4,128)} %param.27) | copy-start | bytes 4612
  23.5 1.5 copy-start.17
  25.0 1.0 copy-start.18
  29.4 1.8 copy-start.4
  32.4 3.2 %collective-permute-start = (f32[264,128]{1,0:T(8,128)S(1)}, f32[264,128]{1,0:T(8,128)S(1)}, u32[]{:S(2)}, u32[]{:S(2)}) collective-permute-start(f32[264,128]{1,0:T(8,128)S(1)} %pad_maximum_fusion), channel_id=1, source_target_pairs={{0,4},{4,0},{8,12},{12,8},{16,20},{20,16},{24,28},{28,24},{32,36},... | collective-permute-start | bytes 405512 | tf_op jit(solution)/shard_map/ppermute | solution.py:58
  36.4 7.7 %collective-permute-start.1 = (f32[264,128]{1,0:T(8,128)S(1)}, f32[264,128]{1,0:T(8,128)S(1)}, u32[]{:S(2)}, u32[]{:S(2)}) collective-permute-start(f32[264,128]{1,0:T(8,128)S(1)} %pad_maximum_fusion.1), channel_id=1, source_target_pairs={{0,8},{4,12},{8,0},{12,4},{16,24},{20,28},{24,16},{28,20},{32,40},... | collective-permute-start | bytes 405512 | tf_op jit(solution)/shard_map/ppermute | solution.py:58
  44.9 11.3 %collective-permute-start.2 = (f32[264,128]{1,0:T(8,128)S(1)}, f32[264,128]{1,0:T(8,128)S(1)}, u32[]{:S(2)}, u32[]{:S(2)}) collective-permute-start(f32[264,128]{1,0:T(8,128)S(1)} %pad_maximum_fusion.2), channel_id=1, source_target_pairs={{0,16},{4,20},{8,24},{12,28},{16,0},{20,4},{24,8},{28,12},{32,48},... | collective-permute-start | bytes 405512 | tf_op jit(solution)/shard_map/ppermute | solution.py:58
  56.9 9.1 %copy-start.5 = (bf16[64,4,128]{2,0,1:T(8,128)(2,1)S(1)}, bf16[64,4,128]{2,0,1:T(8,128)(2,1)}, u32[]{:S(2)}) copy-start(bf16[64,4,128]{2,0,1:T(8,128)(2,1)} %get-tuple-element.41) | copy-start | bytes 196612
  57.0 19.4 %collective-permute-start.3 = (f32[264,128]{1,0:T(8,128)S(1)}, f32[264,128]{1,0:T(8,128)S(1)}, u32[]{:S(2)}, u32[]{:S(2)}) collective-permute-start(f32[264,128]{1,0:T(8,128)S(1)} %pad_maximum_fusion.3), channel_id=1, source_target_pairs={{0,32},{4,36},{8,40},{12,44},{16,48},{20,52},{24,56},{28,60},{32,0... | collective-permute-start | bytes 405512 | tf_op jit(solution)/shard_map/ppermute | solution.py:58
  77.1 13.6 %copy-start.7 = (bf16[64,4,2,64]{3,2,0,1:T(2,128)(2,1)S(1)}, bf16[64,4,2,64]{3,2,0,1:T(2,128)(2,1)}, u32[]{:S(2)}) copy-start(bf16[64,4,2,64]{3,2,0,1:T(2,128)(2,1)} %reshape.249) | copy-start | bytes 196612
  77.1 26.0 %collective-permute-start.4 = (f32[264,128]{1,0:T(8,128)S(1)}, f32[264,128]{1,0:T(8,128)S(1)}, u32[]{:S(2)}, u32[]{:S(2)}) collective-permute-start(f32[264,128]{1,0:T(8,128)S(1)} %pad_maximum_fusion.4), channel_id=1, source_target_pairs={{0,64},{4,68},{8,72},{12,76},{16,80},{20,84},{24,88},{28,92},{32,9... | collective-permute-start | bytes 405512 | tf_op jit(solution)/shard_map/ppermute | solution.py:58
  103.9 7.2 %collective-permute-start.5 = (f32[264,128]{1,0:T(8,128)S(1)}, f32[264,128]{1,0:T(8,128)S(1)}, u32[]{:S(2)}, u32[]{:S(2)}) collective-permute-start(f32[264,128]{1,0:T(8,128)S(1)} %pad_maximum_fusion.5), channel_id=1, source_target_pairs={{0,128},{4,132},{8,136},{12,140},{16,144},{20,148},{24,152},{28,15... | collective-permute-start | bytes 405512 | tf_op jit(solution)/shard_map/ppermute | solution.py:58
  111.9 8.4 %collective-permute-start.6 = (f32[264,128]{1,0:T(8,128)S(1)}, f32[264,128]{1,0:T(8,128)S(1)}, u32[]{:S(2)}, u32[]{:S(2)}) collective-permute-start(f32[264,128]{1,0:T(8,128)S(1)} %pad_maximum_fusion.6), channel_id=1, source_target_pairs={{0,256},{4,260},{8,264},{12,268},{16,272},{20,276},{24,280},{28,28... | collective-permute-start | bytes 405512 | tf_op jit(solution)/shard_map/ppermute | solution.py:58
  125.1 58.4 %copy-start.8 = (f32[1024]{0:T(1024)S(1)}, f32[1024]{0:T(1024)}, u32[]{:S(2)}) copy-start(f32[1024]{0:T(1024)} %param.29) | copy-start | bytes 12292
  125.1 97.8 %reduce-scatter.2.cloned.1.call-start = ((), (), s32[]{:S(2)}) async-start(), calls=%async_computation.2 | async-start | bytes 1310720 | tf_op jit(solution)/shard_map/reduce_scatter | solution.py:156
  183.4 1.5 copy-start.1
  186.0 1.2 copy-start.16
  186.0 1.2 copy-start.19
  190.3 32.6 %copy-start.9 = (f32[1024]{0:T(1024)S(1)}, f32[1024]{0:T(1024)}, u32[]{:S(2)}) copy-start(f32[1024]{0:T(1024)} %param.35) | copy-start | bytes 12292
  222.9 1.1 copy-start.2
  222.9 1.4 copy-start.13
  (5 other events, 3.7 us)
Sparse Core Ops, SparseCore 0:
  125.2 58.1 all-reduce.1
  190.4 32.4 reduce-scatter.1
where the time goes:
time: 233 us
  waiting for transfers between devices  132 us (57%)
  starting transfers between devices  41.2 us (18%)
  local copies, waits for them, and re-layouts  16.8 us (7%)
  between operations  14.3 us (6%)
  blocking collectives  13.1 us (6%)
  matrix products  8.92 us (4%)
  other arithmetic  6.39 us (3%)
    psum x1, waiting for transfers between devices, on_device(): summed = lax.psum(head_terms, 'head')  58.1 us
    ppermute x7, waiting for transfers between devices, seq_merge(): other = lax.ppermute(packed, 'seq', pairs)  41.2 us
    ppermute x7, starting transfers between devices, seq_merge(): other = lax.ppermute(packed, 'seq', pairs)  41 us
    reduce_scatter x1, waiting for transfers between devices, on_device(): lax.psum_scatter(jnp.einsum('rtf,fd->rtd', hidden_all, w_down, preferred_...  32.6 us
    all_gather x1, blocking collectives, on_device(): block_rows = lax.all_gather(tokens, 'head', axis=0, tiled=True)  13.1 us
    unnamed x41, local copies, waits for them, and re-layouts  4.99 us
  transfers between devices with their start and end apart: 9, of which 9 were waited for; matrix products, arithmetic and copies ran while one was open for 0% of the time, Pallas kernels for 0%

commit v1 on v0

--- a/solution.py
+++ b/solution.py
@@ -6,6 +6,19 @@
 HDIM = 64
 NEG = -1e30
 EPS = 1e-05
+
+
+def gather_around(array, axis, dim):
+    ways = lax.axis_size(axis)
+    up = [(d, (d + 1) % ways) for d in range(ways)]
+    down = [(d, (d - 1) % ways) for d in range(ways)]
+    earlier, later = ([array], [array])
+    for _ in range(ways // 2):
+        earlier.append(lax.ppermute(earlier[-1], axis, up))
+    for _ in range((ways - 1) // 2):
+        later.append(lax.ppermute(later[-1], axis, down))
+    line = jnp.concatenate([*earlier[::-1], *later[1:]], axis=dim)
+    return jnp.roll(line, (lax.axis_index(axis) - ways // 2) * array.shape[dim], axis=dim)
 
 
 def layer_norm(values, norm_gain, norm_bias):
@@ -98,7 +111,7 @@
     block_len = cache_keys.shape[1]
     own_rows = tokens.shape[0]
     steps_count = tokens.shape[1]
-    block_rows = lax.all_gather(tokens, "head", axis=0, tiled=True)
+    block_rows = gather_around(tokens, "head", 0)
     triple = (
         jnp.einsum("rtd,kdc->rtkc", block_rows, w_qkv, preferred_element_type=jnp.float32)
         + qkv_bias

time: 233 us -> 237 us (1.017)
  blocking collectives: 13.1 us -> 0 us
  starting transfers between devices: 41.2 us -> 50.5 us
  waiting for transfers between devices: 132 us -> 135 us
    all_gather x1 -> x0, blocking collectives: 13.1 us -> none  [on_device(): block_rows = lax.all_gather(tokens, 'head', axis=0, tiled=True)]
    ppermute x0 -> x3, starting transfers between devices: none -> 9.24 us  [the longest x2 5.59 us: gather_around(): earlier.append(lax.ppermute(earlier[-1], axis, up))]
    ppermute x0 -> x3, waiting for transfers between devices: none -> 5.78 us  [the longest x2 5.78 us: gather_around(): earlier.append(lax.ppermute(earlier[-1], axis, up))]
    unnamed x41 -> x56, local copies, waits for them, and re-layouts: 4.99 us -> 7.25 us
  transfers between devices with their start and end apart: 9 -> 12, of which waited for: 9 -> 10; matrix products, arithmetic and copies ran while one was open for 0% -> 2% of each run, Pallas kernels for 0% -> 0%
where the time goes in v1:
time: 237 us; the launch traced here: 236 us
  waiting for transfers between devices  135 us (57%)
  starting transfers between devices  50.5 us (21%)
  local copies, waits for them, and re-layouts  18.8 us (8%)
  between operations  14.5 us (6%)
  matrix products  11.1 us (5%)
  other arithmetic  5.87 us (2%)
    psum x1, waiting for transfers between devices, on_device(): summed = lax.psum(head_terms, 'head')  55.8 us
    ppermute x7, waiting for transfers between devices, seq_merge(): other = lax.ppermute(packed, 'seq', pairs)  41.2 us
    ppermute x7, starting transfers between devices, seq_merge(): other = lax.ppermute(packed, 'seq', pairs)  41 us
    reduce_scatter x1, waiting for transfers between devices, on_device(): lax.psum_scatter(jnp.einsum('rtf,fd->rtd', hidden_all, w_down, preferred_...  32.6 us
    unnamed x56, local copies, waits for them, and re-layouts  7.25 us
    ppermute x2, waiting for transfers between devices, gather_around(): earlier.append(lax.ppermute(earlier[-1], axis, up))  5.78 us
    ppermute x2, starting transfers between devices, gather_around(): earlier.append(lax.ppermute(earlier[-1], axis, up))  5.59 us
  transfers between devices with their start and end apart: 12, of which 10 were waited for; matrix products, arithmetic and copies ran while one was open for 2% of the time, Pallas kernels for 0%

profile of v1, /device:TPU:8, one launch (start us, length us, event | category | flops | bytes accessed | tf_op | source)
XLA Modules:
  0.0 236.0 jit_solution(14033944574964702933)
XLA Ops:
  7.6 3.4 %collective-permute-start = (bf16[16,4,1024]{2,0,1:T(8,128)(2,1)S(1)}, bf16[16,4,1024]{2,0,1:T(8,128)(2,1)S(1)}, u32[]{:S(2)}, u32[]{:S(2)}) collective-permute-start(bf16[16,4,1024]{2,0,1:T(8,128)(2,1)S(1)} %copy.131), channel_id=1, source_target_pairs={{0,1},{1,2},{2,3},{3,0},{4,5},{5,6},{6,7},{7,4},{8,9},{9,10},{10,1... | collective-permute-start | bytes 393224 | tf_op jit(solution)/shard_map/ppermute | solution.py:17
  11.0 3.7 %collective-permute-start.2 = (bf16[16,4,1024]{2,0,1:T(8,128)(2,1)S(1)}, bf16[16,4,1024]{2,0,1:T(8,128)(2,1)S(1)}, u32[]{:S(2)}, u32[]{:S(2)}) collective-permute-start(bf16[16,4,1024]{2,0,1:T(8,128)(2,1)S(1)} %copy.131), channel_id=1, source_target_pairs={{0,3},{1,0},{2,1},{3,2},{4,7},{5,4},{6,5},{7,6},{8,11},{9,8},{10,9... | collective-permute-start | bytes 393224 | tf_op jit(solution)/shard_map/ppermute | solution.py:19
  16.1 1.5 fusion.8
  20.5 2.2 collective-permute-start.1
  22.8 5.8 %collective-permute-done.1 = bf16[16,4,1024]{2,0,1:T(8,128)(2,1)S(1)} collective-permute-done((bf16[16,4,1024]{2,0,1:T(8,128)(2,1)S(1)}, bf16[16,4,1024]{2,0,1:T(8,128)(2,1)S(1)}, u32[]{:S(2)}, u32[]{:S(2)}) %collective-permute-start.1) | collective-permute-done | bytes 131104 | tf_op jit(solution)/shard_map/ppermute | solution.py:17
  31.9 2.7 %select_reduce_fusion = (f32[64,4,2]{1,2,0:T(2,128)S(1)}, f32[64,4,2,32]{3,1,2,0:T(4,128)}) fusion(pred[64,32]{1,0:T(8,128)(4,1)S(1)} %compare_and_fusion, bf16[64,4,2,64]{3,2,0,1:T(2,128)(2,1)S(1)} %reshape.249, bf16[64,32,2,64]{3,2,1,0:T(2,128)(2,1)} %reshape.247), kind=kOutput, calls=%fused_computation.90 | convolution fusion | flops 2145792 | bytes 659456 | tf_op jit(solution)/shard_map/rthe,rphe->rthp/dot_general | solution.py:45
  35.1 1.4 convert_reduce_fusion
  38.1 1.9 collective-permute-start.3
  42.1 3.8 %collective-permute-start.4 = (f32[264,128]{1,0:T(8,128)S(1)}, f32[264,128]{1,0:T(8,128)S(1)}, u32[]{:S(2)}, u32[]{:S(2)}) collective-permute-start(f32[264,128]{1,0:T(8,128)S(1)} %pad_maximum_fusion.1), channel_id=1, source_target_pairs={{0,8},{4,12},{8,0},{12,4},{16,24},{20,28},{24,16},{28,20},{32,40},... | collective-permute-start | bytes 405512 | tf_op jit(solution)/shard_map/ppermute | solution.py:71
  46.0 3.9 %collective-permute-done.4 = f32[264,128]{1,0:T(8,128)S(1)} collective-permute-done((f32[264,128]{1,0:T(8,128)S(1)}, f32[264,128]{1,0:T(8,128)S(1)}, u32[]{:S(2)}, u32[]{:S(2)}) %collective-permute-start.4) | collective-permute-done | bytes 135200 | tf_op jit(solution)/shard_map/ppermute | solution.py:71
  50.6 5.2 %collective-permute-start.5 = (f32[264,128]{1,0:T(8,128)S(1)}, f32[264,128]{1,0:T(8,128)S(1)}, u32[]{:S(2)}, u32[]{:S(2)}) collective-permute-start(f32[264,128]{1,0:T(8,128)S(1)} %pad_maximum_fusion.2), channel_id=1, source_target_pairs={{0,16},{4,20},{8,24},{12,28},{16,0},{20,4},{24,8},{28,12},{32,48},... | collective-permute-start | bytes 405512 | tf_op jit(solution)/shard_map/ppermute | solution.py:71
  55.8 6.1 %collective-permute-done.5 = f32[264,128]{1,0:T(8,128)S(1)} collective-permute-done((f32[264,128]{1,0:T(8,128)S(1)}, f32[264,128]{1,0:T(8,128)S(1)}, u32[]{:S(2)}, u32[]{:S(2)}) %collective-permute-start.5) | collective-permute-done | bytes 135200 | tf_op jit(solution)/shard_map/ppermute | solution.py:71
  62.7 9.1 %collective-permute-start.6 = (f32[264,128]{1,0:T(8,128)S(1)}, f32[264,128]{1,0:T(8,128)S(1)}, u32[]{:S(2)}, u32[]{:S(2)}) collective-permute-start(f32[264,128]{1,0:T(8,128)S(1)} %pad_maximum_fusion.3), channel_id=1, source_target_pairs={{0,32},{4,36},{8,40},{12,44},{16,48},{20,52},{24,56},{28,60},{32,0... | collective-permute-start | bytes 405512 | tf_op jit(solution)/shard_map/ppermute | solution.py:71
  71.8 10.3 %collective-permute-done.6 = f32[264,128]{1,0:T(8,128)S(1)} collective-permute-done((f32[264,128]{1,0:T(8,128)S(1)}, f32[264,128]{1,0:T(8,128)S(1)}, u32[]{:S(2)}, u32[]{:S(2)}) %collective-permute-start.6) | collective-permute-done | bytes 135200 | tf_op jit(solution)/shard_map/ppermute | solution.py:71
  82.8 13.4 %collective-permute-start.7 = (f32[264,128]{1,0:T(8,128)S(1)}, f32[264,128]{1,0:T(8,128)S(1)}, u32[]{:S(2)}, u32[]{:S(2)}) collective-permute-start(f32[264,128]{1,0:T(8,128)S(1)} %pad_maximum_fusion.4), channel_id=1, source_target_pairs={{0,64},{4,68},{8,72},{12,76},{16,80},{20,84},{24,88},{28,92},{32,9... | collective-permute-start | bytes 405512 | tf_op jit(solution)/shard_map/ppermute | solution.py:71
  96.4 12.3 %collective-permute-done.7 = f32[264,128]{1,0:T(8,128)S(1)} collective-permute-done((f32[264,128]{1,0:T(8,128)S(1)}, f32[264,128]{1,0:T(8,128)S(1)}, u32[]{:S(2)}, u32[]{:S(2)}) %collective-permute-start.7) | collective-permute-done | bytes 135200 | tf_op jit(solution)/shard_map/ppermute | solution.py:71
  109.5 3.7 %collective-permute-start.8 = (f32[264,128]{1,0:T(8,128)S(1)}, f32[264,128]{1,0:T(8,128)S(1)}, u32[]{:S(2)}, u32[]{:S(2)}) collective-permute-start(f32[264,128]{1,0:T(8,128)S(1)} %pad_maximum_fusion.5), channel_id=1, source_target_pairs={{0,128},{4,132},{8,136},{12,140},{16,144},{20,148},{24,152},{28,15... | collective-permute-start | bytes 405512 | tf_op jit(solution)/shard_map/ppermute | solution.py:71
  113.7 3.1 %collective-permute-done.8 = f32[264,128]{1,0:T(8,128)S(1)} collective-permute-done((f32[264,128]{1,0:T(8,128)S(1)}, f32[264,128]{1,0:T(8,128)S(1)}, u32[]{:S(2)}, u32[]{:S(2)}) %collective-permute-start.8) | collective-permute-done | bytes 135200 | tf_op jit(solution)/shard_map/ppermute | solution.py:71
  117.6 3.9 %collective-permute-start.9 = (f32[264,128]{1,0:T(8,128)S(1)}, f32[264,128]{1,0:T(8,128)S(1)}, u32[]{:S(2)}, u32[]{:S(2)}) collective-permute-start(f32[264,128]{1,0:T(8,128)S(1)} %pad_maximum_fusion.6), channel_id=1, source_target_pairs={{0,256},{4,260},{8,264},{12,268},{16,272},{20,276},{24,280},{28,28... | collective-permute-start | bytes 405512 | tf_op jit(solution)/shard_map/ppermute | solution.py:71
  121.9 4.1 %collective-permute-done.9 = f32[264,128]{1,0:T(8,128)S(1)} collective-permute-done((f32[264,128]{1,0:T(8,128)S(1)}, f32[264,128]{1,0:T(8,128)S(1)}, u32[]{:S(2)}, u32[]{:S(2)}) %collective-permute-start.9) | collective-permute-done | bytes 135200 | tf_op jit(solution)/shard_map/ppermute | solution.py:71
  131.0 55.8 %all-reduce.2.cloned.1.call-done = f32[64,4,1024]{2,0,1:T(8,128)} async-done(((f32[64,4,1024]{2,0,1:T(8,128)}), f32[64,4,1024]{2,0,1:T(8,128)}) %all-reduce.2.cloned.1.call-update) | async-done | bytes 1048592 | tf_op jit(solution)/shard_map/psum | solution.py:159
  186.8 1.5 fusion.63
  191.2 2.5 %fusion.9 = f32[64,4,1024]{2,0,1:T(8,128)} fusion(bf16[512,1024]{1,0:T(8,128)(2,1)S(1)} %copy-done, f32[64,4,512]{2,0,1:T(8,128)S(1)} %get-tuple-element.45, u8[64,512]{1,0:T(8,128)(4,1)S(1)} %get-tuple-element.6, u8[64,512]{1,0:T(8,128)(4,1)S(1)} %get-tuple-element.5), kind=kOutput, calls=%fused_computation.16 | convolution fusion | flops 277610496 | bytes 2686976 | tf_op jit(solution)/shard_map/rtf,fd->rtd/dot_general | solution.py:170
  193.7 32.6 %reduce-scatter.2.cloned.1.call-done = f32[16,4,1024]{2,0,1:T(8,128)} async-done(((f32[64,4,1024]{2,0,1:T(8,128)}), f32[16,4,1024]{2,0,1:T(8,128)}) %reduce-scatter.2.cloned.1.call-update) | async-done | bytes 262160 | tf_op jit(solution)/shard_map/reduce_scatter | solution.py:169
  (194 shorter events, 27.7 us)
Async XLA Ops:
  6.5 184.6 %copy-start = (bf16[512,1024]{1,0:T(8,128)(2,1)S(1)}, bf16[512,1024]{1,0:T(8,128)(2,1)}, u32[]{:S(2)}) copy-start(bf16[512,1024]{1,0:T(8,128)(2,1)} %param.34) | copy-start | bytes 3145732
  6.5 180.3 %all-reduce.2.cloned.1.call-start = ((), (), s32[]{:S(2)}) async-start(), calls=%async_computation.1 | async-start | bytes 2097152 | tf_op jit(solution)/shard_map/psum | solution.py:159
  7.6 12.9 %collective-permute-start = (bf16[16,4,1024]{2,0,1:T(8,128)(2,1)S(1)}, bf16[16,4,1024]{2,0,1:T(8,128)(2,1)S(1)}, u32[]{:S(2)}, u32[]{:S(2)}) collective-permute-start(bf16[16,4,1024]{2,0,1:T(8,128)(2,1)S(1)} %copy.131), channel_id=1, source_target_pairs={{0,1},{1,2},{2,3},{3,0},{4,5},{5,6},{6,7},{7,4},{8,9},{9,10},{10,1... | collective-permute-start | bytes 393224 | tf_op jit(solution)/shard_map/ppermute | solution.py:17
  11.0 18.5 %collective-permute-start.2 = (bf16[16,4,1024]{2,0,1:T(8,128)(2,1)S(1)}, bf16[16,4,1024]{2,0,1:T(8,128)(2,1)S(1)}, u32[]{:S(2)}, u32[]{:S(2)}) collective-permute-start(bf16[16,4,1024]{2,0,1:T(8,128)(2,1)S(1)} %copy.131), channel_id=1, source_target_pairs={{0,3},{1,0},{2,1},{3,2},{4,7},{5,4},{6,5},{7,6},{8,11},{9,8},{10,9... | collective-permute-start | bytes 393224 | tf_op jit(solution)/shard_map/ppermute | solution.py:19
  16.1 1.5 copy-start.21
  18.6 1.4 copy-start.5
  20.4 2.2 copy-start.19
  20.5 8.1 %collective-permute-start.1 = (bf16[16,4,1024]{2,0,1:T(8,128)(2,1)S(1)}, bf16[16,4,1024]{2,0,1:T(8,128)(2,1)S(1)}, u32[]{:S(2)}, u32[]{:S(2)}) collective-permute-start(bf16[16,4,1024]{2,0,1:T(8,128)(2,1)S(1)} %collective-permute-done), channel_id=1, source_target_pairs={{0,1},{1,2},{2,3},{3,0},{4,5},{5,6},{6,7},{7,4},{8,9},{9,10},{10,1... | collective-permute-start | bytes 393224 | tf_op jit(solution)/shard_map/ppermute | solution.py:17
  31.9 2.7 %copy-start.9 = (bf16[64,4,2,64]{3,2,0,1:T(2,128)(2,1)}, bf16[64,4,2,64]{3,2,0,1:T(2,128)(2,1)S(1)}, u32[]{:S(2)}) copy-start(bf16[64,4,2,64]{3,2,0,1:T(2,128)(2,1)S(1)} %reshape.249) | copy-start | bytes 196612
  35.1 1.4 copy-start.6
  38.1 3.2 %collective-permute-start.3 = (f32[264,128]{1,0:T(8,128)S(1)}, f32[264,128]{1,0:T(8,128)S(1)}, u32[]{:S(2)}, u32[]{:S(2)}) collective-permute-start(f32[264,128]{1,0:T(8,128)S(1)} %pad_maximum_fusion), channel_id=1, source_target_pairs={{0,4},{4,0},{8,12},{12,8},{16,20},{20,16},{24,28},{28,24},{32,36},... | collective-permute-start | bytes 405512 | tf_op jit(solution)/shard_map/ppermute | solution.py:71
  42.1 7.7 %collective-permute-start.4 = (f32[264,128]{1,0:T(8,128)S(1)}, f32[264,128]{1,0:T(8,128)S(1)}, u32[]{:S(2)}, u32[]{:S(2)}) collective-permute-start(f32[264,128]{1,0:T(8,128)S(1)} %pad_maximum_fusion.1), channel_id=1, source_target_pairs={{0,8},{4,12},{8,0},{12,4},{16,24},{20,28},{24,16},{28,20},{32,40},... | collective-permute-start | bytes 405512 | tf_op jit(solution)/shard_map/ppermute | solution.py:71
  50.6 11.3 %collective-permute-start.5 = (f32[264,128]{1,0:T(8,128)S(1)}, f32[264,128]{1,0:T(8,128)S(1)}, u32[]{:S(2)}, u32[]{:S(2)}) collective-permute-start(f32[264,128]{1,0:T(8,128)S(1)} %pad_maximum_fusion.2), channel_id=1, source_target_pairs={{0,16},{4,20},{8,24},{12,28},{16,0},{20,4},{24,8},{28,12},{32,48},... | collective-permute-start | bytes 405512 | tf_op jit(solution)/shard_map/ppermute | solution.py:71
  62.7 19.4 %collective-permute-start.6 = (f32[264,128]{1,0:T(8,128)S(1)}, f32[264,128]{1,0:T(8,128)S(1)}, u32[]{:S(2)}, u32[]{:S(2)}) collective-permute-start(f32[264,128]{1,0:T(8,128)S(1)} %pad_maximum_fusion.3), channel_id=1, source_target_pairs={{0,32},{4,36},{8,40},{12,44},{16,48},{20,52},{24,56},{28,60},{32,0... | collective-permute-start | bytes 405512 | tf_op jit(solution)/shard_map/ppermute | solution.py:71
  82.8 13.5 %copy-start.7 = (bf16[64,4,128]{2,0,1:T(8,128)(2,1)S(1)}, bf16[64,4,128]{2,0,1:T(8,128)(2,1)}, u32[]{:S(2)}) copy-start(bf16[64,4,128]{2,0,1:T(8,128)(2,1)} %get-tuple-element.41) | copy-start | bytes 196612
  82.8 25.9 %collective-permute-start.7 = (f32[264,128]{1,0:T(8,128)S(1)}, f32[264,128]{1,0:T(8,128)S(1)}, u32[]{:S(2)}, u32[]{:S(2)}) collective-permute-start(f32[264,128]{1,0:T(8,128)S(1)} %pad_maximum_fusion.4), channel_id=1, source_target_pairs={{0,64},{4,68},{8,72},{12,76},{16,80},{20,84},{24,88},{28,92},{32,9... | collective-permute-start | bytes 405512 | tf_op jit(solution)/shard_map/ppermute | solution.py:71
  109.4 3.7 %copy-start.10 = (bf16[64,4,2,64]{3,2,0,1:T(2,128)(2,1)S(1)}, bf16[64,4,2,64]{3,2,0,1:T(2,128)(2,1)}, u32[]{:S(2)}) copy-start(bf16[64,4,2,64]{3,2,0,1:T(2,128)(2,1)} %copy-done.9) | copy-start | bytes 196612
  109.5 7.4 %collective-permute-start.8 = (f32[264,128]{1,0:T(8,128)S(1)}, f32[264,128]{1,0:T(8,128)S(1)}, u32[]{:S(2)}, u32[]{:S(2)}) collective-permute-start(f32[264,128]{1,0:T(8,128)S(1)} %pad_maximum_fusion.5), channel_id=1, source_target_pairs={{0,128},{4,132},{8,136},{12,140},{16,144},{20,148},{24,152},{28,15... | collective-permute-start | bytes 405512 | tf_op jit(solution)/shard_map/ppermute | solution.py:71
  117.6 8.4 %collective-permute-start.9 = (f32[264,128]{1,0:T(8,128)S(1)}, f32[264,128]{1,0:T(8,128)S(1)}, u32[]{:S(2)}, u32[]{:S(2)}) collective-permute-start(f32[264,128]{1,0:T(8,128)S(1)} %pad_maximum_fusion.6), channel_id=1, source_target_pairs={{0,256},{4,260},{8,264},{12,268},{16,272},{20,276},{24,280},{28,28... | collective-permute-start | bytes 405512 | tf_op jit(solution)/shard_map/ppermute | solution.py:71
  130.7 56.1 %copy-start.11 = (f32[1024]{0:T(1024)S(1)}, f32[1024]{0:T(1024)}, u32[]{:S(2)}) copy-start(f32[1024]{0:T(1024)} %param.29) | copy-start | bytes 12292
  130.7 95.5 %reduce-scatter.2.cloned.1.call-start = ((), (), s32[]{:S(2)}) async-start(), calls=%async_computation.2 | async-start | bytes 1310720 | tf_op jit(solution)/shard_map/reduce_scatter | solution.py:169
  186.8 1.5 copy-start.1
  193.7 32.6 %copy-start.12 = (f32[1024]{0:T(1024)S(1)}, f32[1024]{0:T(1024)}, u32[]{:S(2)}) copy-start(f32[1024]{0:T(1024)} %param.35) | copy-start | bytes 12292
  226.3 1.4 copy-start.16
  (12 other events, 11.0 us)
Sparse Core Ops, SparseCore 0:
  130.9 55.8 all-reduce.1
  193.8 32.4 reduce-scatter.1
